TPU v7x, 32 devices: a whole 2x2x4 slice. The times are simulated.
32 devices in a mesh: space: 8 (over y, x, core), species: 4 (over z).
Axes of the slice: x: 2, y: 2, z: 4, core: 2. Of those that a mesh axis runs over, the one named last changes fastest.
Arguments:
- cotangent: bfloat16 [4, 400, 20, 1024], P('species', None, None, 'space'), may hold values from -6 to 6
- freq: float32 [4], P('species'), may hold values from 0.2 to 0.9
- ratio: float32 [4], P('species'), may hold values from 0.5 to 1
- coupling: float32 [4, 4, 13], replicated, may hold values from 0.1 to 0.6
- wall: int32 [1024], P('space'), may hold values 0 or 1
- inlet: int32 [1024], P('space'), may hold values 0 or 1
- face_type: int32 [2, 8], P(None, 'space'), may hold values from 0 to 1
Outputs:
- grad_state: bfloat16 [4, 400, 20, 1024], P('species', None, None, 'space')
Inputs may be any that keep to these rules, and one draw needn't show every extreme that they name: `wall`: 1 marks a solid cell. `inlet`: 1 marks an inlet cell. `face_type`: 0 is a specular wall, 1 a reversing wall.
All inputs are finite; a program needn't handle non-finite values. No bound on the sum of `wall` or of `inlet` on one device may be relied on, other than what follows from the above.
Results may differ from a plain program's by a relative error of at most 0.0049.
Values may be sent and summed in bfloat16 or wider, within the bound.
No kernel may reach another device: no remote copies, remote signals or barrier semaphores. Data moves between devices by JAX's collectives and lax.ppermute only.
A program may use at most 64 MiB of HBM per device.

v0:
```python
import math
import jax
import jax.numpy as jnp
from jax import lax
from jax.sharding import PartitionSpec as P

NZ = 128
courant_max = 0.45
node_reach = 2.85


def passed_along(value, axis, steps):
    count = lax.axis_size(axis)
    pairs = [(source, (source + steps) % count) for source in range(count)]
    return lax.ppermute(value, axis, pairs)


def velocity_tables(node_count):
    pair_count = node_count * node_count
    spacing = 2.0 * node_reach / (node_count - 1)
    node_line = (
        jnp.arange(node_count, dtype=jnp.int32).astype(jnp.float32) - 0.5 * (node_count - 1)
    ) * spacing
    grid_shape = (pair_count, node_count)
    along_x = jnp.broadcast_to(jnp.repeat(node_line, node_count)[:, None], grid_shape)
    along_y = jnp.broadcast_to(jnp.tile(node_line, node_count)[:, None], grid_shape)
    along_z = jnp.broadcast_to(node_line[None, :], grid_shape)
    square = along_x * along_x + along_y * along_y + along_z * along_z
    heat_term = square - 2.5
    functions = [
        jnp.ones(grid_shape, jnp.float32),
        along_x,
        along_y,
        along_z,
        square - 1.5,
        along_x * along_y,
        along_x * along_z,
        along_y * along_z,
        along_x * along_x - along_y * along_y,
        along_y * along_y - along_z * along_z,
        along_x * heat_term,
        along_y * heat_term,
        along_z * heat_term,
    ]
    stacked = jnp.stack(functions).reshape(len(functions), pair_count * node_count)
    basis_table = stacked / jnp.sqrt(jnp.mean(stacked * stacked, axis=1, keepdims=True))
    weights = jnp.exp(-square).reshape(-1) * (spacing * spacing * spacing) / math.pi**1.5
    recon_table = basis_table * weights[None, :]
    return (node_line, basis_table, recon_table)


def keep_factor(wall, inlet, pair_count):
    upward = (jnp.arange(pair_count, dtype=jnp.int32) >= pair_count // 2).astype(jnp.float32)
    open_cells = (1 - wall).astype(jnp.float32)
    inflow = inlet.astype(jnp.float32)
    return open_cells[None, None, :] * (1.0 - upward[:, None, None] * inflow[None, None, :])


def on_device(cotangent, freq, ratio, coupling, wall, inlet, face_type):
    pair_count = cotangent.shape[1]
    node_count = cotangent.shape[2]
    cell_count = cotangent.shape[3]
    depth_cells = NZ
    column_count = cell_count // depth_cells
    half_pairs = pair_count // 2
    node_line, basis_table, recon_table = velocity_tables(node_count)
    keep_mask = keep_factor(wall, inlet, pair_count)
    masked = cotangent[0] * keep_mask.astype(jnp.bfloat16)
    moments = jnp.dot(
        basis_table,
        masked.reshape(pair_count * node_count, cell_count),
        precision=lax.Precision.HIGHEST,
        preferred_element_type=jnp.float32,
    )
    species_index = lax.axis_index("species")
    rate_value = freq[0]
    row_k = lax.dynamic_index_in_dim(coupling, species_index, axis=0, keepdims=False)
    cross_terms = jnp.sum(
        row_k[:, :, None] * lax.all_gather(moments[None], "species", axis=0, tiled=True), axis=0
    )
    rebuilt = jnp.dot(
        recon_table.T,
        cross_terms,
        precision=lax.Precision.HIGHEST,
        preferred_element_type=jnp.float32,
    ).reshape(pair_count, node_count, cell_count)
    relaxed = ((1.0 - rate_value) * masked.astype(jnp.float32) + rebuilt).astype(jnp.bfloat16)
    rim_shape = (half_pairs, node_count, depth_cells)
    zero_half = jnp.zeros(rim_shape, jnp.bfloat16)
    first_upper = relaxed[half_pairs:, :, :depth_cells].reshape(
        half_pairs, node_count * depth_cells
    )
    got_next = passed_along(first_upper, "space", -1).reshape(rim_shape)
    last_lower = relaxed[:half_pairs, :, cell_count - depth_cells :].reshape(
        half_pairs, node_count * depth_cells
    )
    got_prev = passed_along(last_lower, "space", 1).reshape(rim_shape)
    next_rim = jnp.concatenate([zero_half, got_next], axis=0)
    prev_rim = jnp.concatenate([got_prev, zero_half], axis=0)
    field = relaxed.astype(jnp.float32).reshape(pair_count, node_count, column_count, depth_cells)
    scale_factor = courant_max * ratio[0] / node_reach
    adv_x = (scale_factor * jnp.repeat(node_line, node_count))[:, None, None, None]
    adv_z = (scale_factor * node_line)[None, :, None, None]
    plus_x = jnp.maximum(adv_x, 0.0)
    minus_x = jnp.maximum(-adv_x, 0.0)
    plus_z = jnp.maximum(adv_z, 0.0)
    minus_z = jnp.maximum(-adv_z, 0.0)
    shifted_up_x = jnp.concatenate(
        [field[:, :, 1:], next_rim.astype(jnp.float32)[:, :, None, :]], axis=2
    )
    shifted_down_x = jnp.concatenate(
        [prev_rim.astype(jnp.float32)[:, :, None, :], field[:, :, : column_count - 1]], axis=2
    )
    zero_plane = jnp.zeros_like(field[..., :1])
    upper_z = jnp.concatenate([field[..., 1:], zero_plane], axis=3)
    lower_z = jnp.concatenate([zero_plane, field[..., :-1]], axis=3)
    result = (1.0 - jnp.abs(adv_x) - jnp.abs(adv_z)) * field
    result = result + plus_x * shifted_up_x + minus_x * shifted_down_x
    result = result + plus_z * upper_z + minus_z * lower_z
    bottom_part = plus_z[..., 0] * field[..., 0]
    bottom_add = jnp.where(
        face_type[0][None, None, :] == 1,
        jnp.flip(bottom_part, axis=(0, 1)),
        jnp.flip(bottom_part, axis=1),
    )
    top_part = minus_z[..., 0] * field[..., depth_cells - 1]
    top_add = jnp.where(
        face_type[1][None, None, :] == 1,
        jnp.flip(top_part, axis=(0, 1)),
        jnp.flip(top_part, axis=1),
    )
    result = result.at[..., 0].add(bottom_add)
    result = result.at[..., depth_cells - 1].add(top_add)
    return result.reshape(pair_count, node_count, cell_count).astype(jnp.bfloat16)[None]


def solution(mesh):
    in_specs = (
        P("species", None, None, "space"),
        P("species"),
        P("species"),
        P(),
        P("space"),
        P("space"),
        P(None, "space"),
    )
    out_specs = P("species", None, None, "space")
    return jax.shard_map(
        on_device, mesh=mesh, in_specs=in_specs, out_specs=out_specs, check_vma=False
    )
```

profile of v0, /device:TPU:1, one launch (start us, length us, event | category | flops | bytes accessed | tf_op | source)
XLA Modules:
  0.0 108.2 jit_solution(7815667221158033408)
XLA Ops:
  6.1 2.8 %dot_general.11 = f32[400,20,13]{1,0,2:T(8,128)S(1)} reshape(f32[8000,13]{0,1:T(8,128)} %multiply_bitcast_fusion) | data formatting | bytes 832000 | tf_op jit(solution)/shard_map/dot_general | solution.py:81
  9.0 2.7 %copy.47 = f32[400,20,13]{0,2,1:T(8,128)} copy(f32[400,20,13]{1,0,2:T(8,128)S(1)} %dot_general.11) | data formatting | bytes 832000 | tf_op jit(solution)/shard_map/dot_general | solution.py:81
  12.4 2.2 %copy.45 = bf16[1,400,20,128]{3,2,1,0:T(8,128)(2,1)S(1)} copy(bf16[1,400,20,128]{3,1,2,0:T(8,128)(2,1)} %param.11) | data formatting | bytes 4096000 | tf_op args[0]
  14.5 2.0 %squeeze.18 = bf16[8000,128]{1,0:T(8,128)(2,1)} reshape(bf16[1,400,20,128]{3,2,1,0:T(8,128)(2,1)S(1)} %copy.45) | data formatting | bytes 4096000 | tf_op jit(solution)/shard_map/squeeze | solution.py:68
  17.0 2.0 %mul.363 = bf16[8000,128]{1,0:T(8,128)(2,1)} reshape(bf16[400,20,128]{2,1,0:T(8,128)(2,1)S(1)} %mul.346.clone) | data formatting | bytes 4096000 | tf_op jit(solution)/shard_map/mul | solution.py:68
  19.0 3.3 %fusion.8 = f32[1,13,128]{2,1,0:T(8,128)S(1)} fusion(bf16[8000,128]{1,0:T(8,128)(2,1)} %squeeze.18, bf16[8000,128]{1,0:T(8,128)(2,1)} %mul.363, f32[13,8000]{1,0:T(8,128)S(1)} %stack.24, f32[13]{0:T(128)S(1)} %multiply_sqrt_fusion), kind=kOutput, calls=%fused_computation.17 | convolution fusion | flops 160872000 | bytes 4518708 | tf_op jit(solution)/shard_map/dot_general | solution.py:69
  22.3 11.6 %all-gather.1 = f32[4,13,128]{2,1,0:T(8,128)S(1)} all-gather(f32[1,13,128]{2,1,0:T(8,128)S(1)} %fusion.8), channel_id=2, replica_groups=mesh['space'=8,'species'=4] {'species'}, dimensions={0}, use_global_device_ids=true | all-gather | bytes 33280 | tf_op jit(solution)/shard_map/all_gather | solution.py:79
  34.0 8.1 %add_convert_fusion = bf16[400,20,128]{2,0,1:T(8,128)(2,1)S(1)} fusion(f32[400,20,13]{0,2,1:T(8,128)} %copy.47, bf16[1,400,20,128]{3,1,2,0:T(8,128)(2,1)} %param.11, f32[]{:T(128)} %bitcast.2, bf16[400,128]{1,0:T(8,128)(2,1)S(1)} %multiply_convert_fusion, f32[13,128]{1,0:T(8,128)S(1)} %multiply_reduce_fusion.1), kind=kOutput, calls=%fused_computation.12 | convolution fusion | flops 164864000 | bytes 4621060 | tf_op jit(solution)/shard_map/dot_general | solution.py:81
  42.5 4.4 %collective-permute-start.1 = (bf16[200,2560]{1,0:T(8,128)(2,1)S(1)}, bf16[200,2560]{1,0:T(8,128)(2,1)}, u32[]{:S(2)}, u32[]{:S(2)}) collective-permute-start(bf16[200,2560]{1,0:T(8,128)(2,1)S(1)} %bitcast.71), channel_id=1, source_target_pairs={{0,4},{4,8},{8,12},{12,16},{16,20},{20,24},{24,28},{28,0},{1,5},{5... | collective-permute-start | bytes 3072008 | tf_op jit(solution)/shard_map/ppermute | solution.py:15
  46.9 1.1 %copy.65 = bf16[20,25,8,128]{3,2,0,1:T(8,128)(2,1)} copy(bf16[20,25,8,128]{3,2,1,0:T(8,128)(2,1)S(1)} %get-tuple-element.35) | data formatting | bytes 2048000 | tf_op jit(solution)/shard_map/reshape | solution.py:90
  49.1 3.8 %slice_reduce_fusion = (f32[400,20]{0,1:T(8,128)S(1)}, f32[400,20]{0,1:T(8,128)S(1)}) fusion(f32[400,20,1,128]{3,0,1,2:T(8,128)S(1)} %convert_bitcast_fusion), kind=kLoop, calls=%fused_computation.7 | loop fusion | bytes 128000 | tf_op jit(solution)/shard_map/slice | solution.py:126
  54.3 2.7 %copy.52 = f32[400,20,1,1]{3,0,1,2:T(8,128)} copy(f32[400,20,1,1]{0,2,1,3:T(1,128)S(1)} %fusion.11) | data formatting | bytes 64000 | tf_op jit(solution)/shard_map/reshape.57
  58.4 2.7 %copy.53 = f32[400,20,1,1]{3,0,1,2:T(8,128)} copy(f32[400,20,1,1]{0,2,1,3:T(1,128)S(1)} %fusion.12) | data formatting | bytes 64000 | tf_op jit(solution)/shard_map/reshape.68
  61.2 4.7 %fusion.22 = (f32[400,20,1,127]{3,0,1,2:T(8,128)S(1)}, f32[400,20,1,127]{3,0,1,2:T(8,128)S(1)}) fusion(f32[400,20,1,128]{3,0,1,2:T(8,128)} %copy-done.1), kind=kLoop, calls=%fused_computation.60 | loop fusion | bytes 16256000 | tf_op jit(solution)/shard_map/slice | solution.py:115
  66.3 1.4 %copy_bitcast_fusion.2 = bf16[200,20,128]{2,0,1:T(8,128)(2,1)S(1)} fusion(bf16[200,2560]{1,0:T(8,128)(2,1)} %collective-permute-done.1), kind=kLoop, calls=%fused_computation.20 | loop fusion | bytes 2048000 | tf_op jit(solution)/shard_map/reshape | solution.py:97
  67.6 3.4 %collective-permute-done = bf16[200,2560]{1,0:T(8,128)(2,1)} collective-permute-done((bf16[200,2560]{1,0:T(8,128)(2,1)}, bf16[200,2560]{1,0:T(8,128)(2,1)}, u32[]{:S(2)}, u32[]{:S(2)}) %collective-permute-start) | collective-permute-done | bytes 1024032 | tf_op jit(solution)/shard_map/ppermute | solution.py:15
  71.1 1.4 %copy_bitcast_fusion.3 = bf16[200,20,128]{2,0,1:T(8,128)(2,1)S(1)} fusion(bf16[200,2560]{1,0:T(8,128)(2,1)} %collective-permute-done), kind=kLoop, calls=%fused_computation.21 | loop fusion | bytes 2048000 | tf_op jit(solution)/shard_map/reshape | solution.py:93
  72.5 3.1 %fusion.4 = f32[400,20,1,128]{3,0,1,2:T(8,128)S(1)} fusion(bf16[400,20,128]{2,0,1:T(8,128)(2,1)S(1)} %add_convert_fusion, f32[400,20,1,127]{3,0,1,2:T(8,128)S(1)} %get-tuple-element.34, f32[400,20,1,127]{3,0,1,2:T(8,128)S(1)} %get-tuple-element.33, f32[20]{0:T(128)S(1)} %get-tuple-element.56, f32[20]{0:T(128)S(1)} %get-tuple-element.57, ...), kind=kLoop, calls=%fused_computation.6 | loop fusion | flops 12288000 | bytes 16355360 | tf_op jit(solution)/shard_map/add | solution.py:119
  75.6 1.9 %copy-done.2 = f32[400,20,1,128]{3,0,1,2:T(8,128)} copy-done((f32[400,20,1,128]{3,0,1,2:T(8,128)}, f32[400,20,1,128]{3,0,1,2:T(8,128)S(1)}, u32[]{:S(2)}) %copy-start.2) | copy-done | bytes 4096024
  77.5 2.4 %slice_add_fusion.1 = f32[400,20,1,1]{3,0,1,2:T(8,128)} fusion(f32[400,20,1,1]{3,0,1,2:T(8,128)S(1)} %copy-done.3, f32[400,20,1,128]{3,0,1,2:T(8,128)S(1)} %fusion.4), kind=kLoop, calls=%fused_computation.11 | loop fusion | flops 8000 | bytes 96000 | tf_op jit(solution)/shard_map/add | solution.py:132
  79.8 8.3 %scatter-add.6 = f32[400,20,1,128]{3,0,1,2:T(8,128)} dynamic-update-slice(f32[400,20,1,128]{3,0,1,2:T(8,128)} %copy-done.2, f32[400,20,1,1]{3,0,1,2:T(8,128)} %slice_add_fusion.1, s32[]{:T(128)} %constant.110.clone.1, s32[]{:T(128)} %constant.110.clone.1, s32[]{:T(128)} %constant.110.clone.1, s32[]{:T(128)} %constant.110.clone.1) | dynamic-update-slice | bytes 64004 | tf_op jit(solution)/shard_map/scatter-add | solution.py:132
  88.1 6.5 %fusion.5 = f32[400,20,1]{2,0,1:T(8,128)} fusion(f32[400,20,1,1]{3,0,1,2:T(8,128)} %copy.53, f32[400,20,1,128]{3,0,1,2:T(8,128)} %scatter-add.6), kind=kLoop, calls=%fused_computation.9 | loop fusion | flops 8000 | bytes 96000 | tf_op jit(solution)/shard_map/reshape | solution.py:134
  94.6 9.9 %scatter-add.9 = f32[400,20,128]{2,0,1:T(8,128)} dynamic-update-slice(f32[400,20,128]{2,0,1:T(8,128)} %bitcast.70, f32[400,20,1]{2,0,1:T(8,128)} %fusion.5, s32[]{:T(128)} %constant.110.clone.1, s32[]{:T(128)} %constant.110.clone.1, s32[]{:T(128)} %constant.114.clone.1) | dynamic-update-slice | bytes 64004 | tf_op jit(solution)/shard_map/scatter-add | solution.py:133
  104.4 3.7 %convert_bitcast_fusion.1 = bf16[1,400,20,128]{3,1,2,0:T(8,128)(2,1)} fusion(f32[400,20,128]{2,0,1:T(8,128)} %scatter-add.9), kind=kLoop, calls=%fused_computation.14 | loop fusion | flops 1024000 | bytes 6144000 | tf_op jit(solution)/shard_map/broadcast_in_dim | solution.py:134
  (71 shorter events, 9.1 us)
Async XLA Ops:
  0.0 33.9 %copy-start = (f32[4,4,13]{2,1,0:T(4,128)S(1)}, f32[4,4,13]{2,1,0:T(4,128)}, u32[]{:S(2)}) copy-start(f32[4,4,13]{2,1,0:T(4,128)} %param.14) | copy-start | bytes 2500
  5.0 7.3 %copy-start.5 = (s32[128]{0:T(128)S(1)}, s32[128]{0:T(128)}, u32[]{:S(2)}) copy-start(s32[128]{0:T(128)} %param.16) | copy-start | bytes 1540
  5.0 7.3 %copy-start.6 = (s32[128]{0:T(128)S(1)}, s32[128]{0:T(128)}, u32[]{:S(2)}) copy-start(s32[128]{0:T(128)} %param.15) | copy-start | bytes 1540
  42.5 23.8 %collective-permute-start.1 = (bf16[200,2560]{1,0:T(8,128)(2,1)S(1)}, bf16[200,2560]{1,0:T(8,128)(2,1)}, u32[]{:S(2)}, u32[]{:S(2)}) collective-permute-start(bf16[200,2560]{1,0:T(8,128)(2,1)S(1)} %bitcast.71), channel_id=1, source_target_pairs={{0,4},{4,8},{8,12},{12,16},{16,20},{20,24},{24,28},{28,0},{1,5},{5... | collective-permute-start | bytes 3072008 | tf_op jit(solution)/shard_map/ppermute | solution.py:15
  46.9 1.4 %copy-start.4 = (s32[2,1]{0,1:T(1,128)S(1)}, s32[2,1]{0,1:T(1,128)}, u32[]{:S(2)}) copy-start(s32[2,1]{0,1:T(1,128)} %param.17) | copy-start | bytes 28
  48.0 23.1 %collective-permute-start = (bf16[200,2560]{1,0:T(8,128)(2,1)}, bf16[200,2560]{1,0:T(8,128)(2,1)}, u32[]{:S(2)}, u32[]{:S(2)}) collective-permute-start(bf16[200,2560]{1,0:T(8,128)(2,1)} %bitcast.69), channel_id=1, source_target_pairs={{0,28},{4,0},{8,4},{12,8},{16,12},{20,16},{24,20},{28,24},{1,29},{... | collective-permute-start | bytes 3072008 | tf_op jit(solution)/shard_map/ppermute | solution.py:15
  48.3 4.6 %copy-start.1 = (f32[400,20,1,128]{3,0,1,2:T(8,128)}, f32[400,20,1,128]{3,0,1,2:T(8,128)S(1)}, u32[]{:S(2)}) copy-start(f32[400,20,1,128]{3,0,1,2:T(8,128)S(1)} %convert_bitcast_fusion) | copy-start | bytes 12288004
  72.5 5.0 %copy-start.3 = (f32[400,20,1,1]{3,0,1,2:T(8,128)S(1)}, f32[400,20,1,1]{3,0,1,2:T(8,128)}, u32[]{:S(2)}) copy-start(f32[400,20,1,1]{3,0,1,2:T(8,128)} %copy.52) | copy-start | bytes 96004
  75.6 1.9 %copy-start.2 = (f32[400,20,1,128]{3,0,1,2:T(8,128)}, f32[400,20,1,128]{3,0,1,2:T(8,128)S(1)}, u32[]{:S(2)}) copy-start(f32[400,20,1,128]{3,0,1,2:T(8,128)S(1)} %fusion.4) | copy-start | bytes 12288004
where the time goes:
time: 109 us; the launch traced here: 108 us
  local copies, waits for them, and re-layouts  55.8 us (51%)
  other arithmetic  18.1 us (17%)
  blocking collectives  11.6 us (11%)
  matrix products  11.4 us (10%)
  starting transfers between devices  4.42 us (4%)
  waiting for transfers between devices  3.78 us (3%)
  between operations  3.02 us (3%)
    all_gather x1, blocking collectives, on_device(): lax.all_gather(moments[None], 'species', axis=0, tiled=True)  11.6 us
    scatter-add x1, local copies, waits for them, and re-layouts, on_device(): result = result.at[..., depth_cells - 1].add(top_add)  9.88 us
    scatter-add x1, local copies, waits for them, and re-layouts, on_device(): result = result.at[..., 0].add(bottom_add)  8.28 us
    dot_general x1, matrix products, on_device(): jnp.dot(recon_table.T, cross_terms, precision=lax.Precision.HIGHEST, pref...  8.12 us
    reshape x1, other arithmetic, on_device(): result.reshape(pair_count, node_count, cell_count).astype(jnp.bfloat16)  6.46 us
    dot_general x2, local copies, waits for them, and re-layouts, on_device(): jnp.dot(recon_table.T, cross_terms, precision=lax.Precision.HIGHEST, pref...  5.52 us
    another operation x2, local copies, waits for them, and re-layouts  5.33 us
    unnamed x18, local copies, waits for them, and re-layouts  5.31 us
  transfers between devices with their start and end apart: 2, of which 2 were waited for; matrix products, arithmetic and copies ran while one was open for 18% of the time, Pallas kernels for 0%

commit v1 on v0

--- a/solution.py
+++ b/solution.py
@@ -76,7 +76,12 @@
     rate_value = freq[0]
     row_k = lax.dynamic_index_in_dim(coupling, species_index, axis=0, keepdims=False)
     cross_terms = jnp.sum(
-        row_k[:, :, None] * lax.all_gather(moments[None], "species", axis=0, tiled=True), axis=0
+        row_k[:, :, None]
+        * jnp.concatenate(
+            lax.all_to_all(jnp.stack([moments[None]] * lax.axis_size("species")), "species", 0, 0),
+            axis=0,
+        ),
+        axis=0,
     )
     rebuilt = jnp.dot(
         recon_table.T,

time: 109 us -> 103 us (0.945)
  blocking collectives: 11.6 us -> 0 us
  starting transfers between devices: 4.42 us -> 7.52 us
  waiting for transfers between devices: 3.78 us -> 6.13 us
    all_gather x1 -> x0, blocking collectives: 11.6 us -> none  [on_device(): lax.all_gather(moments[None], 'species', axis=0, tiled=True)]
    all_to_all x0 -> x1, starting transfers between devices: none -> 5.41 us  [on_device(): lax.all_to_all(jnp.stack([moments[None]] * lax.axis_size('species')), 'sp...]
    ppermute x2, waiting for transfers between devices: 3.78 us -> 6.13 us  [passed_along(): return lax.ppermute(value, axis, pairs)]
    ppermute x2, starting transfers between devices: 4.42 us -> 2.11 us  [passed_along(): return lax.ppermute(value, axis, pairs)]
    dot_general x2, local copies, waits for them, and re-layouts: 5.52 us -> 3.73 us  [on_device(): jnp.dot(recon_table.T, cross_terms, precision=lax.Precision.HIGHEST, pref...]
    unnamed x18 -> x26, local copies, waits for them, and re-layouts: 5.31 us -> 5.99 us
    another operation x2 -> x3, local copies, waits for them, and re-layouts: 5.33 us -> 5.96 us
  transfers between devices with their start and end apart: 2 -> 3, of which waited for: 2 -> 2; matrix products, arithmetic and copies ran while one was open for 18% -> 23% of each run, Pallas kernels for 0% -> 0%
where the time goes in v1:
time: 103 us
  local copies, waits for them, and re-layouts  55.3 us (54%)
  other arithmetic  19.1 us (19%)
  matrix products  11.3 us (11%)
  starting transfers between devices  7.52 us (7%)
  waiting for transfers between devices  6.13 us (6%)
  between operations  3.1 us (3%)
    scatter-add x1, local copies, waits for them, and re-layouts, on_device(): result = result.at[..., depth_cells - 1].add(top_add)  9.89 us
    scatter-add x1, local copies, waits for them, and re-layouts, on_device(): result = result.at[..., 0].add(bottom_add)  8.26 us
    dot_general x1, matrix products, on_device(): jnp.dot(recon_table.T, cross_terms, precision=lax.Precision.HIGHEST, pref...  8.03 us
    reshape x1, other arithmetic, on_device(): result.reshape(pair_count, node_count, cell_count).astype(jnp.bfloat16)  6.43 us
    ppermute x2, waiting for transfers between devices, passed_along(): return lax.ppermute(value, axis, pairs)  6.13 us
    unnamed x26, local copies, waits for them, and re-layouts  5.99 us
    all_to_all x1, starting transfers between devices, on_device(): lax.all_to_all(jnp.stack([moments[None]] * lax.axis_size('species')), 'sp...  5.41 us
    another operation x2, local copies, waits for them, and re-layouts  5.33 us
  transfers between devices with their start and end apart: 3, of which 2 were waited for; matrix products, arithmetic and copies ran while one was open for 23% of the time, Pallas kernels for 0%

profile of v1, /device:TPU:1, one launch (start us, length us, event | category | flops | bytes accessed | tf_op | source)
XLA Modules:
  0.0 102.6 jit_solution(1605385045028398546)
XLA Ops:
  5.6 2.2 %copy.56 = bf16[1,400,20,128]{3,2,1,0:T(8,128)(2,1)S(1)} copy(bf16[1,400,20,128]{3,1,2,0:T(8,128)(2,1)} %param.11) | data formatting | bytes 4096000 | tf_op args[0]
  7.7 2.0 %squeeze.18 = bf16[8000,128]{1,0:T(8,128)(2,1)} reshape(bf16[1,400,20,128]{3,2,1,0:T(8,128)(2,1)S(1)} %copy.56) | data formatting | bytes 4096000 | tf_op jit(solution)/shard_map/squeeze | solution.py:68
  10.8 2.1 %mul.363 = bf16[8000,128]{1,0:T(8,128)(2,1)} reshape(bf16[400,20,128]{2,1,0:T(8,128)(2,1)S(1)} %mul.346.clone) | data formatting | bytes 4096000 | tf_op jit(solution)/shard_map/mul | solution.py:68
  12.8 3.3 %fusion.6 = f32[13,128]{1,0:T(8,128)S(1)} fusion(bf16[8000,128]{1,0:T(8,128)(2,1)} %squeeze.18, bf16[8000,128]{1,0:T(8,128)(2,1)} %mul.363, f32[13,8000]{1,0:T(8,128)S(1)} %stack.27, f32[13]{0:T(128)S(1)} %multiply_sqrt_fusion), kind=kOutput, calls=%fused_computation.15 | convolution fusion | flops 160872000 | bytes 4518708 | tf_op jit(solution)/shard_map/dot_general | solution.py:69
  16.8 5.4 %all-to-all-start = ((f32[4,1,13,128]{3,1,2,0:T(1,128)}), f32[4,1,13,128]{3,1,2,0:T(1,128)}, u32[]{:S(2)}, u32[]{:S(2)}) async-start(f32[4,1,13,128]{3,1,2,0:T(1,128)} %stack.28), calls=%async_computation | async-start | bytes 53248 | tf_op jit(solution)/shard_map/all_to_all | solution.py:81
  23.9 1.8 %dot_general.11 = f32[400,20,13]{1,0,2:T(8,128)S(1)} reshape(f32[8000,13]{0,1:T(8,128)S(1)} %multiply_bitcast_fusion) | data formatting | bytes 832000 | tf_op jit(solution)/shard_map/dot_general | solution.py:86
  25.7 2.0 %copy.59 = f32[400,20,13]{0,2,1:T(8,128)S(1)} copy(f32[400,20,13]{1,0,2:T(8,128)S(1)} %dot_general.11) | data formatting | bytes 832000 | tf_op jit(solution)/shard_map/dot_general | solution.py:86
  30.5 8.0 %add_convert_fusion = bf16[400,20,128]{2,0,1:T(8,128)(2,1)S(1)} fusion(f32[400,20,13]{0,2,1:T(8,128)S(1)} %copy.59, bf16[1,400,20,128]{3,1,2,0:T(8,128)(2,1)} %param.11, f32[]{:T(128)} %bitcast.2, bf16[400,128]{1,0:T(8,128)(2,1)} %copy-done.4, f32[13,128]{1,0:T(8,128)S(1)} %fusion.10), kind=kOutput, calls=%fused_computation.12 | convolution fusion | flops 164864000 | bytes 4621060 | tf_op jit(solution)/shard_map/dot_general | solution.py:86
  39.2 2.1 %collective-permute-start.1 = (bf16[200,2560]{1,0:T(8,128)(2,1)S(1)}, bf16[200,2560]{1,0:T(8,128)(2,1)}, u32[]{:S(2)}, u32[]{:S(2)}) collective-permute-start(bf16[200,2560]{1,0:T(8,128)(2,1)S(1)} %bitcast.73), channel_id=1, source_target_pairs={{0,4},{4,8},{8,12},{12,16},{16,20},{20,24},{24,28},{28,0},{1,5},{5... | collective-permute-start | bytes 3072008 | tf_op jit(solution)/shard_map/ppermute | solution.py:15
  42.4 3.8 %slice_reduce_fusion = (f32[400,20]{0,1:T(8,128)S(1)}, f32[400,20]{0,1:T(8,128)S(1)}) fusion(f32[400,20,1,128]{3,0,1,2:T(8,128)S(1)} %convert_bitcast_fusion), kind=kLoop, calls=%fused_computation.7 | loop fusion | bytes 128000 | tf_op jit(solution)/shard_map/slice | solution.py:131
  47.1 2.7 %copy.64 = f32[400,20,1,1]{3,0,1,2:T(8,128)} copy(f32[400,20,1,1]{0,2,1,3:T(1,128)S(1)} %fusion.8) | data formatting | bytes 64000 | tf_op jit(solution)/shard_map/reshape.58
  50.6 2.6 %copy.65 = f32[400,20,1,1]{3,0,1,2:T(8,128)} copy(f32[400,20,1,1]{0,2,1,3:T(1,128)S(1)} %fusion.9) | data formatting | bytes 64000 | tf_op jit(solution)/shard_map/reshape.69
  53.2 4.7 %fusion.20 = (f32[400,20,1,127]{3,0,1,2:T(8,128)S(1)}, f32[400,20,1,127]{3,0,1,2:T(8,128)S(1)}) fusion(f32[400,20,1,128]{3,0,1,2:T(8,128)} %copy-done.1), kind=kLoop, calls=%fused_computation.60 | loop fusion | bytes 16256000 | tf_op jit(solution)/shard_map/slice | solution.py:120
  57.9 2.7 %collective-permute-done.1 = bf16[200,2560]{1,0:T(8,128)(2,1)} collective-permute-done((bf16[200,2560]{1,0:T(8,128)(2,1)S(1)}, bf16[200,2560]{1,0:T(8,128)(2,1)}, u32[]{:S(2)}, u32[]{:S(2)}) %collective-permute-start.1) | collective-permute-done | bytes 1024032 | tf_op jit(solution)/shard_map/ppermute | solution.py:15
  60.6 1.4 %copy_bitcast_fusion.2 = bf16[200,20,128]{2,0,1:T(8,128)(2,1)S(1)} fusion(bf16[200,2560]{1,0:T(8,128)(2,1)} %collective-permute-done.1), kind=kLoop, calls=%fused_computation.19 | loop fusion | bytes 2048000 | tf_op jit(solution)/shard_map/reshape | solution.py:102
  62.0 3.4 %collective-permute-done = bf16[200,2560]{1,0:T(8,128)(2,1)} collective-permute-done((bf16[200,2560]{1,0:T(8,128)(2,1)}, bf16[200,2560]{1,0:T(8,128)(2,1)}, u32[]{:S(2)}, u32[]{:S(2)}) %collective-permute-start) | collective-permute-done | bytes 1024032 | tf_op jit(solution)/shard_map/ppermute | solution.py:15
  65.5 1.4 %copy_bitcast_fusion.3 = bf16[200,20,128]{2,0,1:T(8,128)(2,1)S(1)} fusion(bf16[200,2560]{1,0:T(8,128)(2,1)} %collective-permute-done), kind=kLoop, calls=%fused_computation.20 | loop fusion | bytes 2048000 | tf_op jit(solution)/shard_map/reshape | solution.py:98
  66.9 3.1 %fusion.4 = f32[400,20,1,128]{3,0,1,2:T(8,128)S(1)} fusion(bf16[400,20,128]{2,0,1:T(8,128)(2,1)S(1)} %add_convert_fusion, f32[400,20,1,127]{3,0,1,2:T(8,128)S(1)} %get-tuple-element.34, f32[400,20,1,127]{3,0,1,2:T(8,128)S(1)} %get-tuple-element.33, f32[20]{0:T(128)S(1)} %get-tuple-element.56, f32[20]{0:T(128)S(1)} %copy-done.7, ...), kind=kLoop, calls=%fused_computation.6 | loop fusion | flops 12288000 | bytes 16355360 | tf_op jit(solution)/shard_map/add | solution.py:124
  70.0 1.9 %copy-done.2 = f32[400,20,1,128]{3,0,1,2:T(8,128)} copy-done((f32[400,20,1,128]{3,0,1,2:T(8,128)}, f32[400,20,1,128]{3,0,1,2:T(8,128)S(1)}, u32[]{:S(2)}) %copy-start.2) | copy-done | bytes 4096024
  71.9 2.3 %slice_add_fusion.1 = f32[400,20,1,1]{3,0,1,2:T(8,128)} fusion(f32[400,20,1,1]{3,0,1,2:T(8,128)S(1)} %copy-done.3, f32[400,20,1,128]{3,0,1,2:T(8,128)S(1)} %fusion.4), kind=kLoop, calls=%fused_computation.11 | loop fusion | flops 8000 | bytes 96000 | tf_op jit(solution)/shard_map/add | solution.py:137
  74.3 8.3 %scatter-add.6 = f32[400,20,1,128]{3,0,1,2:T(8,128)} dynamic-update-slice(f32[400,20,1,128]{3,0,1,2:T(8,128)} %copy-done.2, f32[400,20,1,1]{3,0,1,2:T(8,128)} %slice_add_fusion.1, s32[]{:T(128)} %constant.110.clone.1, s32[]{:T(128)} %constant.110.clone.1, s32[]{:T(128)} %constant.110.clone.1, s32[]{:T(128)} %constant.110.clone.1) | dynamic-update-slice | bytes 64004 | tf_op jit(solution)/shard_map/scatter-add | solution.py:137
  82.5 6.4 %fusion.5 = f32[400,20,1]{2,0,1:T(8,128)} fusion(f32[400,20,1,1]{3,0,1,2:T(8,128)} %copy.65, f32[400,20,1,128]{3,0,1,2:T(8,128)} %scatter-add.6), kind=kLoop, calls=%fused_computation.9 | loop fusion | flops 8000 | bytes 96000 | tf_op jit(solution)/shard_map/reshape | solution.py:139
  89.0 9.9 %scatter-add.9 = f32[400,20,128]{2,0,1:T(8,128)} dynamic-update-slice(f32[400,20,128]{2,0,1:T(8,128)} %bitcast.72, f32[400,20,1]{2,0,1:T(8,128)} %fusion.5, s32[]{:T(128)} %constant.110.clone.1, s32[]{:T(128)} %constant.110.clone.1, s32[]{:T(128)} %constant.114.clone.1) | dynamic-update-slice | bytes 64004 | tf_op jit(solution)/shard_map/scatter-add | solution.py:138
  98.8 3.7 %convert_bitcast_fusion.1 = bf16[1,400,20,128]{3,1,2,0:T(8,128)(2,1)} fusion(f32[400,20,128]{2,0,1:T(8,128)} %scatter-add.9), kind=kLoop, calls=%fused_computation.14 | loop fusion | flops 1024000 | bytes 6144000 | tf_op jit(solution)/shard_map/broadcast_in_dim | solution.py:139
  (82 shorter events, 12.2 us)
Async XLA Ops:
  0.0 23.3 %copy-start = (f32[4,4,13]{2,1,0:T(4,128)S(1)}, f32[4,4,13]{2,1,0:T(4,128)}, u32[]{:S(2)}) copy-start(f32[4,4,13]{2,1,0:T(4,128)} %param.14) | copy-start | bytes 2500
  0.0 5.5 %copy-start.9 = (s32[128]{0:T(128)S(1)}, s32[128]{0:T(128)}, u32[]{:S(2)}) copy-start(s32[128]{0:T(128)} %param.16) | copy-start | bytes 1540
  0.0 5.5 %copy-start.10 = (s32[128]{0:T(128)S(1)}, s32[128]{0:T(128)}, u32[]{:S(2)}) copy-start(s32[128]{0:T(128)} %param.15) | copy-start | bytes 1540
  9.8 0.6 copy-start.4
  12.8 9.8 %copy-start.8 = (s32[2,1]{0,1:T(1,128)S(1)}, s32[2,1]{0,1:T(1,128)}, u32[]{:S(2)}) copy-start(s32[2,1]{0,1:T(1,128)} %param.17) | copy-start | bytes 28
  16.8 12.8 %all-to-all-start = ((f32[4,1,13,128]{3,1,2,0:T(1,128)}), f32[4,1,13,128]{3,1,2,0:T(1,128)}, u32[]{:S(2)}, u32[]{:S(2)}) async-start(f32[4,1,13,128]{3,1,2,0:T(1,128)} %stack.28), calls=%async_computation | async-start | bytes 53248 | tf_op jit(solution)/shard_map/all_to_all | solution.py:81
  38.8 3.6 %copy-start.1 = (f32[400,20,1,128]{3,0,1,2:T(8,128)}, f32[400,20,1,128]{3,0,1,2:T(8,128)S(1)}, u32[]{:S(2)}) copy-start(f32[400,20,1,128]{3,0,1,2:T(8,128)S(1)} %convert_bitcast_fusion) | copy-start | bytes 12288004
  39.2 21.5 %collective-permute-start.1 = (bf16[200,2560]{1,0:T(8,128)(2,1)S(1)}, bf16[200,2560]{1,0:T(8,128)(2,1)}, u32[]{:S(2)}, u32[]{:S(2)}) collective-permute-start(bf16[200,2560]{1,0:T(8,128)(2,1)S(1)} %bitcast.73), channel_id=1, source_target_pairs={{0,4},{4,8},{8,12},{12,16},{16,20},{20,24},{24,28},{28,0},{1,5},{5... | collective-permute-start | bytes 3072008 | tf_op jit(solution)/shard_map/ppermute | solution.py:15
  42.4 3.9 %copy-start.7 = (f32[20]{0:T(128)S(1)}, f32[20]{0:T(128)}, u32[]{:S(2)}) copy-start(f32[20]{0:T(128)} %get-tuple-element.57) | copy-start | bytes 244
  42.4 23.1 %collective-permute-start = (bf16[200,2560]{1,0:T(8,128)(2,1)}, bf16[200,2560]{1,0:T(8,128)(2,1)}, u32[]{:S(2)}, u32[]{:S(2)}) collective-permute-start(bf16[200,2560]{1,0:T(8,128)(2,1)} %bitcast.71), channel_id=1, source_target_pairs={{0,28},{4,0},{8,4},{12,8},{16,12},{20,16},{24,20},{28,24},{1,29},{... | collective-permute-start | bytes 3072008 | tf_op jit(solution)/shard_map/ppermute | solution.py:15
  57.9 8.9 %copy-start.5 = (f32[400]{0:T(512)S(1)}, f32[400]{0:T(512)}, u32[]{:S(2)}) copy-start(f32[400]{0:T(512)} %get-tuple-element.48) | copy-start | bytes 4804
  57.9 8.9 %copy-start.6 = (f32[400]{0:T(512)S(1)}, f32[400]{0:T(512)}, u32[]{:S(2)}) copy-start(f32[400]{0:T(512)} %get-tuple-element.49) | copy-start | bytes 4804
  66.9 5.0 %copy-start.3 = (f32[400,20,1,1]{3,0,1,2:T(8,128)S(1)}, f32[400,20,1,1]{3,0,1,2:T(8,128)}, u32[]{:S(2)}) copy-start(f32[400,20,1,1]{3,0,1,2:T(8,128)} %copy.64) | copy-start | bytes 96004
  70.0 1.9 %copy-start.2 = (f32[400,20,1,128]{3,0,1,2:T(8,128)}, f32[400,20,1,128]{3,0,1,2:T(8,128)S(1)}, u32[]{:S(2)}) copy-start(f32[400,20,1,128]{3,0,1,2:T(8,128)S(1)} %fusion.4) | copy-start | bytes 12288004
